TPU v7x, 128 devices: a whole 4x4x4 slice. The times are simulated.
128 devices in a mesh: dp: 4 (over x), seq: 8 (over z, core), expert: 4 (over y).
Axes of the slice: x: 4, y: 4, z: 4, core: 2. Of those that a mesh axis runs over, the one named last changes fastest.
Arguments:
- x_in: bfloat16 [4096, 8192], P(('dp', 'seq'), 'expert'), parts along dimension 0, may hold values from -6 to 6
- z_in: bfloat16 [4096, 8192], P(('dp', 'seq'), 'expert'), parts along dimension 0, may hold values from -6 to 6
- step_raw: bfloat16 [4096, 8192], P(('dp', 'seq'), 'expert'), parts along dimension 0, may hold values from -4 to 4
- step_bias: float32 [8192], P('expert'), may hold values from -9 to -2
- decay_rate: float32 [16, 8192], P(None, 'expert'), may hold values from 0.5 to 4
- b_coef: bfloat16 [16, 4096], P(None, ('dp', 'seq')), parts along dimension 1, may hold values from -6 to 6
- c_coef: bfloat16 [16, 4096], P(None, ('dp', 'seq')), parts along dimension 1, may hold values from -6 to 6
- skip_gain: float32 [8192], P('expert'), may hold values from 0.5 to 1.5
- out_proj: bfloat16 [8192, 8192], P('expert', 'seq'), may hold values from -0.0625 to 0.0625
- residual: bfloat16 [4096, 8192], P(('dp', 'seq', 'expert')), parts along dimension 0, may hold values from -6 to 6
- norm_gain: float32 [8192], replicated, may hold values from 0.5 to 1.5
- router_weight: bfloat16 [8192, 16], replicated, may hold values from -0.0625 to 0.0625
- expert_ids: int32 [4096, 2], P(('dp', 'seq', 'expert')), parts along dimension 0, may hold values from 0 to 15, as said below
- gate_weight: bfloat16 [8192, 12288], P(None, ('seq', 'expert')), may hold values from -0.0625 to 0.0625
- up_weight: bfloat16 [8192, 12288], P(None, ('seq', 'expert')), may hold values from -0.0625 to 0.0625
- down_weight: bfloat16 [12288, 8192], P(('seq', 'expert')), may hold values from -0.0546875 to 0.0546875
Outputs:
- final: bfloat16 [4096, 8192], P(('dp', 'seq', 'expert')), parts along dimension 0
There are 4 independent parts, one for each index of `dp`. A program takes and returns all parts, laid end to end along the dimension named above; an argument that names none is the same for every part. Nothing has to cross between parts.
Inputs may be any that keep to these rules, and one draw needn't show every extreme that they name: `expert_ids`: each token names 2 different experts; among the 32 rows of one device at most 16 name expert 0 and at least one does; on some device exactly 16 do.
All inputs are finite; a program needn't handle non-finite values.
Results may differ from a plain program's by a relative error of at most 0.006.
Values may be sent and summed in bfloat16 or wider, within the bound.
No kernel may reach another device: no remote copies, remote signals or barrier semaphores. Data moves between devices by JAX's collectives and lax.ppermute only.
A program may use at most 192 MiB of HBM per device.

v0:
```python
import jax
import jax.numpy as jnp
from jax import lax
from jax.sharding import PartitionSpec as P

BLOCK = 128


def entering(value, axis, join, neutral):
    count, mine = (lax.axis_size(axis), lax.axis_index(axis))
    stacked = lax.all_gather(jnp.stack(value), axis)
    running = tuple((jnp.full_like(part, zero) for part, zero in zip(value, neutral)))
    for position in range(count - 1):
        longer = join(running, (stacked[position, 0], stacked[position, 1]))
        running = tuple((jnp.where(position < mine, new, old) for new, old in zip(longer, running)))
    return running


def pair_combine(early, later):
    return (early[0] * later[0], later[0] * early[1] + later[1])


def end_state(step_size, x_float, decay_rate, b_rows):

    def end_advance(state, inputs):
        step_now, x_now, b_now = inputs
        state = (
            jnp.exp(-step_now[None, :] * decay_rate) * state
            + (step_now * x_now)[None, :] * b_now[:, None]
        )
        return (state, None)

    start_state = jnp.zeros(decay_rate.shape, jnp.float32)
    final_state, _ = lax.scan(end_advance, start_state, (step_size, x_float, b_rows), unroll=8)
    return final_state


def scan_outputs(state_in, step_size, x_float, decay_rate, b_rows, c_rows, skip_gain):

    def scan_advance(state, inputs):
        step_now, x_now, b_now, c_now = inputs
        state = (
            jnp.exp(-step_now[None, :] * decay_rate) * state
            + (step_now * x_now)[None, :] * b_now[:, None]
        )
        y_now = jnp.sum(c_now[:, None] * state, axis=0) + skip_gain * x_now
        return (state, y_now)

    _, outputs = lax.scan(scan_advance, state_in, (step_size, x_float, b_rows, c_rows), unroll=8)
    return outputs


def on_device(
    x_in,
    z_in,
    step_raw,
    step_bias,
    decay_rate,
    b_coef,
    c_coef,
    skip_gain,
    out_proj,
    residual,
    norm_gain,
    router_weight,
    expert_ids,
    gate_weight,
    up_weight,
    down_weight,
):
    step_size = jax.nn.softplus(step_raw.astype(jnp.float32) + step_bias[None, :])
    x_float = x_in.astype(jnp.float32)
    b_rows = b_coef.astype(jnp.float32).T
    c_rows = c_coef.astype(jnp.float32).T
    state_end = end_state(step_size, x_float, decay_rate, b_rows)
    decay_end = jnp.exp(-decay_rate * jnp.sum(step_size, axis=0)[None, :])
    identity = (1.0, 0.0)
    carried = entering((decay_end, state_end), "seq", pair_combine, identity)
    state_in = carried[1]
    scanned = scan_outputs(state_in, step_size, x_float, decay_rate, b_rows, c_rows, skip_gain)
    gated = (scanned * jax.nn.silu(z_in.astype(jnp.float32))).astype(jnp.bfloat16)
    seq_count = lax.axis_size("seq")
    expert_count = lax.axis_size("expert")
    rows = residual.shape[0]
    gathered = lax.all_gather(gated, "seq", axis=0, tiled=True)
    gathered = gathered.reshape(seq_count, expert_count, rows, gated.shape[1])
    gathered = jnp.transpose(gathered, (1, 0, 2, 3)).reshape(-1, gated.shape[1])
    column_part = jnp.dot(gathered, out_proj, preferred_element_type=jnp.float32)
    summed = lax.psum_scatter(column_part, "expert", scatter_dimension=0, tiled=True)
    summed = summed.reshape(seq_count, rows, column_part.shape[1])
    swapped = lax.all_to_all(summed, "seq", split_axis=0, concat_axis=0, tiled=True)
    mamba_out = jnp.transpose(swapped, (1, 0, 2)).reshape(rows, -1)
    hidden = (residual.astype(jnp.float32) + mamba_out).astype(jnp.bfloat16)
    hidden_f = hidden.astype(jnp.float32)
    width_d = hidden.shape[1]
    scale_cols = width_d // BLOCK
    normed = (
        hidden_f
        * lax.rsqrt(jnp.mean(hidden_f * hidden_f, axis=-1, keepdims=True) + 1e-05)
        * norm_gain[None, :]
    )
    blocked = normed.reshape(rows, scale_cols, BLOCK)
    scales = (jnp.max(jnp.abs(blocked), axis=-1) / 448.0 + 1e-06).astype(jnp.bfloat16)
    quant = (blocked / scales.astype(jnp.float32)[..., None]).astype(jnp.bfloat16)
    restored = (
        (quant.astype(jnp.float32) * scales.astype(jnp.float32)[..., None])
        .astype(jnp.bfloat16)
        .reshape(rows, width_d)
    )
    experts = router_weight.shape[1]
    probs = jax.nn.sigmoid(jnp.dot(restored, router_weight, preferred_element_type=jnp.float32))
    picks = expert_ids[:, :, None] == jnp.arange(experts, dtype=jnp.int32)[None, None, :]
    chosen = jnp.sum(jnp.where(picks, probs[:, None, :], jnp.float32(0.0)), axis=-1)
    weights = chosen / jnp.sum(chosen, axis=-1, keepdims=True)
    coef = jnp.sum(jnp.where(expert_ids == 0, weights, jnp.float32(0.0)), axis=1)
    wanted = jnp.any(expert_ids == 0, axis=1)
    wanted_int = wanted.astype(jnp.int32)
    slot_pos = jnp.cumsum(wanted_int) - wanted_int
    capacity = rows // 2
    table = (
        (slot_pos[None, :] == jnp.arange(capacity, dtype=jnp.int32)[:, None]) & wanted[None, :]
    ).astype(jnp.bfloat16)
    send_rows = jnp.dot(table, restored, preferred_element_type=jnp.float32).astype(jnp.bfloat16)
    inputs = lax.all_gather(send_rows, ("seq", "expert"), axis=0, tiled=True)
    gate_value = jnp.dot(inputs, gate_weight, preferred_element_type=jnp.float32)
    up_value = jnp.dot(inputs, up_weight, preferred_element_type=jnp.float32)
    active = (jax.nn.silu(gate_value) * up_value).astype(jnp.bfloat16)
    own_sum = lax.psum_scatter(
        jnp.dot(active, down_weight, preferred_element_type=jnp.float32).astype(jnp.bfloat16),
        ("seq", "expert"),
        scatter_dimension=0,
        tiled=True,
    )
    returned = jnp.dot(table.T, own_sum, preferred_element_type=jnp.float32)
    return (hidden_f + coef[:, None] * returned).astype(jnp.bfloat16)


def solution(mesh):
    return jax.shard_map(
        on_device,
        mesh=mesh,
        in_specs=(
            P(("dp", "seq"), "expert"),
            P(("dp", "seq"), "expert"),
            P(("dp", "seq"), "expert"),
            P("expert"),
            P(None, "expert"),
            P(None, ("dp", "seq")),
            P(None, ("dp", "seq")),
            P("expert"),
            P("expert", "seq"),
            P(("dp", "seq", "expert"), None),
            P(),
            P(),
            P(("dp", "seq", "expert"), None),
            P(None, ("seq", "expert")),
            P(None, ("seq", "expert")),
            P(("seq", "expert"), None),
        ),
        out_specs=P(("dp", "seq", "expert"), None),
        check_vma=False,
    )
```

profile of v0, /device:TPU:0, one launch (start us, length us, event | category | flops | bytes accessed | tf_op | source)
XLA Modules:
  0.0 427.4 jit_solution(3741020597015307561)
XLA Ops:
  8.5 1.7 fusion.66
  10.2 21.7 %while.24 = (s32[]{:T(128)}, f32[16,2048]{1,0:T(8,128)S(1)}, f32[16,8,2048]{2,1,0:T(8,128)S(1)}, f32[16,2048]{1,0:T(8,128)}, f32[16,8,2048]{2,1,0:T(8,128)S(1)},...) while((s32[]{:T(128)}, f32[16,2048]{1,0:T(8,128)S(1)}, ...), condition=%wide.region_2.3_spmd.clone, body=%wide.region_1.2_spmd.clone.sunk | while | flops 1114122 | bytes 789271 | solution.py:34
  33.9 28.0 %all-gather.9.cloned.1.call-done = f32[16,16,2048]{2,1,0:T(8,128)} async-done(((f32[2,16,2048]{2,1,0:T(8,128)}), f32[16,16,2048]{2,1,0:T(8,128)}) %all-gather.9.cloned.1.call-update) | async-done | bytes 2097168 | tf_op jit(solution)/shard_map/all_gather | solution.py:11
  61.8 1.6 fusion.69
  63.5 71.3 %while.23 = (s32[]{:T(128)}, f32[16,2048]{1,0:T(8,128)S(1)}, f32[16,8,2048]{2,1,0:T(8,128)}, f32[16,8,2048]{2,1,0:T(8,128)S(1)}, f32[16,2048]{1,0:T(8,128)}, /*i...) while((s32[]{:T(128)}, f32[16,2048]{1,0:T(8,128)S(1)}, ...), condition=%wide.region_12.13_spmd, body=%wide.region_3.12_spmd.sunk | while | flops 2408457 | bytes 2078409 | solution.py:49
  64.8 1.2 multiply_reduce_fusion.11
  69.2 1.2 multiply_reduce_fusion.11
  73.7 1.2 multiply_reduce_fusion.11
  78.1 1.2 multiply_reduce_fusion.11
  82.6 1.2 multiply_reduce_fusion.11
  87.0 1.2 multiply_reduce_fusion.11
  91.5 1.2 multiply_reduce_fusion.11
  95.9 1.2 multiply_reduce_fusion.11
  100.4 1.2 multiply_reduce_fusion.11
  104.8 1.2 multiply_reduce_fusion.11
  109.3 1.2 multiply_reduce_fusion.11
  113.7 1.2 multiply_reduce_fusion.11
  118.2 1.2 multiply_reduce_fusion.11
  122.7 1.2 multiply_reduce_fusion.11
  127.1 1.2 multiply_reduce_fusion.11
  134.8 2.3 fusion.64
  137.2 32.6 %all-gather.5.cloned.1.call-done = bf16[1024,2048]{1,0:T(8,128)(2,1)} async-done(((bf16[128,2048]{1,0:T(8,128)(2,1)}), bf16[1024,2048]{1,0:T(8,128)(2,1)}) %all-gather.5.cloned.1.call-update) | async-done | bytes 4194320 | tf_op jit(solution)/shard_map/all_gather | solution.py:85
  169.8 2.7 copy.45
  173.2 6.0 %fusion.99 = f32[1024,1024]{1,0:T(8,128)} fusion(bf16[1024,2048]{1,0:T(8,128)(2,1)S(1)} %bitcast.416, bf16[2048,1024]{1,0:T(8,128)(2,1)S(1)} %copy-done.7), kind=kOutput, calls=%fused_computation.223 | convolution fusion | flops 4294967296 | bytes 12582912 | tf_op jit(solution)/shard_map/dot_general | solution.py:88
  179.3 46.8 %reduce-scatter.3.cloned.1.call-done = f32[256,1024]{1,0:T(8,128)} async-done(((f32[1024,1024]{1,0:T(8,128)}), f32[256,1024]{1,0:T(8,128)}) %reduce-scatter.3.cloned.1.call-update) | async-done | bytes 1048592 | tf_op jit(solution)/shard_map/reduce_scatter | solution.py:89
  226.1 4.4 %all-to-all-start = ((f32[8,32,1024]{2,1,0:T(8,128)}), f32[8,32,1024]{2,1,0:T(8,128)S(1)}, u32[]{:S(2)}, u32[]{:S(2)}) async-start(f32[8,32,1024]{2,1,0:T(8,128)} %bitcast.444), calls=%async_computation.1 | async-start | bytes 2097152 | tf_op jit(solution)/shard_map/all_to_all | solution.py:91
  230.9 15.6 %all-to-all-done = f32[8,32,1024]{2,1,0:T(8,128)S(1)} async-done(((f32[8,32,1024]{2,1,0:T(8,128)}), f32[8,32,1024]{2,1,0:T(8,128)S(1)}, u32[]{:S(2)}, u32[]{:S(2)}) %all-to-all-start) | async-done | bytes 1048608 | tf_op jit(solution)/shard_map/all_to_all | solution.py:91
  249.8 50.5 %all-gather.7.cloned.1.call-done = bf16[512,8192]{1,0:T(8,128)(2,1)} async-done(((bf16[16,8192]{1,0:T(8,128)(2,1)}), bf16[512,8192]{1,0:T(8,128)(2,1)}) %all-gather.7.cloned.1.call-update) | async-done | bytes 8388624 | tf_op jit(solution)/shard_map/all_gather | solution.py:124
  300.3 8.8 %fusion.100 = f32[512,384]{1,0:T(8,128)S(1)} fusion(bf16[512,8192]{1,0:T(8,128)(2,1)} %all-gather.7.cloned.1.call-done, bf16[8192,384]{1,0:T(8,128)(2,1)} %param.33), kind=kOutput, calls=%fused_computation.224 | convolution fusion | flops 3221225472 | bytes 15466496 | tf_op jit(solution)/shard_map/dot_general | solution.py:125
  309.1 17.1 %convolution_convert_fusion = bf16[512,8192]{1,0:T(8,128)(2,1)} fusion(bf16[384,8192]{1,0:T(8,128)(2,1)} %param.35, bf16[512,8192]{1,0:T(8,128)(2,1)} %all-gather.7.cloned.1.call-done, bf16[8192,384]{1,0:T(8,128)(2,1)} %param.34, f32[512,384]{1,0:T(8,128)S(1)} %fusion.100), kind=kOutput, calls=%fused_computation.132 | convolution fusion | flops 6447824896 | bytes 30146560 | tf_op jit(solution)/shard_map/dot_general | solution.py:129
  326.5 92.3 %reduce-scatter.5.cloned.1.call-done = bf16[16,8192]{1,0:T(8,128)(2,1)} async-done(((bf16[512,8192]{1,0:T(8,128)(2,1)}), bf16[16,8192]{1,0:T(8,128)(2,1)}) %reduce-scatter.5.cloned.1.call-update) | async-done | bytes 262160 | tf_op jit(solution)/shard_map/reduce_scatter | solution.py:128
  418.8 2.1 fusion.48
  (263 shorter events, 82.1 us)
Async XLA Ops:
  6.5 319.7 %copy-start = (bf16[8192,16]{0,1:T(8,128)(2,1)S(1)}, bf16[8192,16]{0,1:T(8,128)(2,1)}, u32[]{:S(2)}) copy-start(bf16[8192,16]{0,1:T(8,128)(2,1)} %param.31) | copy-start | bytes 786436
  6.5 27.2 %copy-start.5 = (bf16[16,128]{1,0:T(8,128)(2,1)S(1)}, bf16[16,128]{1,0:T(8,128)(2,1)}, u32[]{:S(2)}) copy-start(bf16[16,128]{1,0:T(8,128)(2,1)} %param.26) | copy-start | bytes 12292
  6.5 56.9 %copy-start.3 = (f32[2048]{0:T(1024)S(1)}, f32[2048]{0:T(1024)}, u32[]{:S(2)}) copy-start(f32[2048]{0:T(1024)} %param.27) | copy-start | bytes 24580
  6.5 55.3 %all-gather.9.cloned.1.call-start = ((), (), s32[]{:S(2)}) async-start(), calls=%async_computation.7 | async-start | bytes 2359296 | tf_op jit(solution)/shard_map/all_gather | solution.py:11
  33.7 136.1 %all-gather.5.cloned.1.call-start = ((), (), s32[]{:S(2)}) async-start(), calls=%async_computation.3 | async-start | bytes 4718592 | tf_op jit(solution)/shard_map/all_gather | solution.py:85
  63.5 71.3 %copy-start.2 = (bf16[128,2048]{1,0:T(8,128)(2,1)S(1)}, bf16[128,2048]{1,0:T(8,128)(2,1)}, u32[]{:S(2)}) copy-start(bf16[128,2048]{1,0:T(8,128)(2,1)} %param.21) | copy-start | bytes 1572868
  137.1 89.0 %reduce-scatter.3.cloned.1.call-start = ((), (), s32[]{:S(2)}) async-start(), calls=%async_computation.4 | async-start | bytes 5242880 | tf_op jit(solution)/shard_map/reduce_scatter | solution.py:89
  169.8 3.4 copy-start.7
  179.2 51.3 %copy-start.6 = (s32[32,2]{0,1:T(2,128)S(1)}, s32[32,2]{0,1:T(2,128)}, u32[]{:S(2)}) copy-start(s32[32,2]{0,1:T(2,128)} %param.32) | copy-start | bytes 772
  179.2 67.3 %copy-start.1 = (bf16[32,8192]{1,0:T(8,128)(2,1)S(1)}, bf16[32,8192]{1,0:T(8,128)(2,1)}, u32[]{:S(2)}) copy-start(bf16[32,8192]{1,0:T(8,128)(2,1)} %param.29) | copy-start | bytes 1572868
  179.2 67.6 %copy-start.4 = (f32[8192]{0:T(1024)S(1)}, f32[8192]{0:T(1024)}, u32[]{:S(2)}) copy-start(f32[8192]{0:T(1024)} %param.30) | copy-start | bytes 98308
  226.1 20.4 %all-to-all-start = ((f32[8,32,1024]{2,1,0:T(8,128)}), f32[8,32,1024]{2,1,0:T(8,128)S(1)}, u32[]{:S(2)}, u32[]{:S(2)}) async-start(f32[8,32,1024]{2,1,0:T(8,128)} %bitcast.444), calls=%async_computation.1 | async-start | bytes 2097152 | tf_op jit(solution)/shard_map/all_to_all | solution.py:91
  230.5 69.8 %all-gather.7.cloned.1.call-start = ((), (), s32[]{:S(2)}) async-start(), calls=%async_computation.5 | async-start | bytes 8650752 | tf_op jit(solution)/shard_map/all_gather | solution.py:124
  249.5 169.3 %reduce-scatter.5.cloned.1.call-start = ((), (), s32[]{:S(2)}) async-start(), calls=%async_computation.6 | async-start | bytes 8650752 | tf_op jit(solution)/shard_map/reduce_scatter | solution.py:128
Sparse Core Ops, SparseCore 0:
  33.8 27.9 all-gather.8
  137.2 32.4 all-gather.4
  179.4 46.6 reduce-scatter.2
  249.7 50.5 all-gather.6
  326.3 92.4 reduce-scatter.4
where the time goes:
time: 429 us; the launch traced here: 427 us
  waiting for transfers between devices  266 us (62%)
  other arithmetic  90.4 us (21%)
  matrix products  35.2 us (8%)
  local copies, waits for them, and re-layouts  16.7 us (4%)
  between operations  13.3 us (3%)
  starting transfers between devices  4.79 us (1%)
    reduce_scatter x1, waiting for transfers between devices, on_device(): lax.psum_scatter(jnp.dot(active, down_weight, preferred_element_type=jnp....  92.3 us
    reduce_sum x48, other arithmetic, scan_advance(): y_now = jnp.sum(c_now[:, None] * state, axis=0) + skip_gain * x_now  54.9 us
    all_gather x1, waiting for transfers between devices, on_device(): inputs = lax.all_gather(send_rows, ('seq', 'expert'), axis=0, tiled=True)  50.5 us
    reduce_scatter x1, waiting for transfers between devices, on_device(): lax.psum_scatter(column_part, 'expert', scatter_dimension=0, tiled=True)  46.8 us
    all_gather x1, waiting for transfers between devices, on_device(): gathered = lax.all_gather(gated, 'seq', axis=0, tiled=True)  32.6 us
    all_gather x1, waiting for transfers between devices, entering(): stacked = lax.all_gather(jnp.stack(value), axis)  28 us
    add x16, other arithmetic, end_advance(): jnp.exp(-step_now[None, :] * decay_rate) * state  18.6 us
    dot_general x1, matrix products, on_device(): jnp.dot(active, down_weight, preferred_element_type=jnp.float32)  17.1 us
  transfers between devices with their start and end apart: 6, of which 6 were waited for; matrix products, arithmetic and copies ran while one was open for 0% of the time, Pallas kernels for 0%

commit v1 on v0

--- a/solution.py
+++ b/solution.py
@@ -4,6 +4,14 @@
 from jax.sharding import PartitionSpec as P
 
 BLOCK = 128
+
+
+def cut_counts(v0, d0):
+    local_now = jnp.stack(tuple((v0 for _ in range(lax.axis_size("seq")))))
+    u_next = jnp.concatenate(
+        lax.all_to_all(local_now, axis_name="seq", split_axis=0, concat_axis=0), d0
+    )
+    return u_next
 
 
 def entering(value, axis, join, neutral):
@@ -82,7 +90,7 @@
     seq_count = lax.axis_size("seq")
     expert_count = lax.axis_size("expert")
     rows = residual.shape[0]
-    gathered = lax.all_gather(gated, "seq", axis=0, tiled=True)
+    gathered = cut_counts(gated, 0)
     gathered = gathered.reshape(seq_count, expert_count, rows, gated.shape[1])
     gathered = jnp.transpose(gathered, (1, 0, 2, 3)).reshape(-1, gated.shape[1])
     column_part = jnp.dot(gathered, out_proj, preferred_element_type=jnp.float32)

time: 429 us -> 447 us (1.042)
  blocking collectives: 0 us -> 52.9 us
  waiting for transfers between devices: 266 us -> 233 us
    all_to_all x0 -> x1, blocking collectives: none -> 52.9 us  [cut_counts(): lax.all_to_all(local_now, axis_name='seq', split_axis=0, concat_axis=0)]
    all_gather x1 -> x0, waiting for transfers between devices: 32.6 us -> none  [on_device(): gathered = lax.all_gather(gated, 'seq', axis=0, tiled=True)]
  transfers between devices with their start and end apart: 6 -> 5, of which waited for: 6 -> 5; matrix products, arithmetic and copies ran while one was open for 0% -> 0% of each run, Pallas kernels for 0% -> 0%
where the time goes in v1:
time: 447 us; the launch traced here: 446 us
  waiting for transfers between devices  233 us (52%)
  other arithmetic  89.7 us (20%)
  blocking collectives  52.9 us (12%)
  matrix products  35.2 us (8%)
  local copies, waits for them, and re-layouts  16 us (4%)
  between operations  13.3 us (3%)
  starting transfers between devices  4.72 us (1%)
    reduce_scatter x1, waiting for transfers between devices, on_device(): lax.psum_scatter(jnp.dot(active, down_weight, preferred_element_type=jnp....  92.3 us
    reduce_sum x48, other arithmetic, scan_advance(): y_now = jnp.sum(c_now[:, None] * state, axis=0) + skip_gain * x_now  54.9 us
    all_to_all x1, blocking collectives, cut_counts(): lax.all_to_all(local_now, axis_name='seq', split_axis=0, concat_axis=0)  52.9 us
    all_gather x1, waiting for transfers between devices, on_device(): inputs = lax.all_gather(send_rows, ('seq', 'expert'), axis=0, tiled=True)  50.5 us
    reduce_scatter x1, waiting for transfers between devices, on_device(): lax.psum_scatter(column_part, 'expert', scatter_dimension=0, tiled=True)  46.3 us
    all_gather x1, waiting for transfers between devices, entering(): stacked = lax.all_gather(jnp.stack(value), axis)  28 us
    add x16, other arithmetic, end_advance(): jnp.exp(-step_now[None, :] * decay_rate) * state  18.7 us
    dot_general x1, matrix products, on_device(): jnp.dot(active, down_weight, preferred_element_type=jnp.float32)  17.1 us
  transfers between devices with their start and end apart: 5, of which 5 were waited for; matrix products, arithmetic and copies ran while one was open for 0% of the time, Pallas kernels for 0%

profile of v1, /device:TPU:0, one launch (start us, length us, event | category | flops | bytes accessed | tf_op | source)
XLA Modules:
  0.0 445.7 jit_solution(11347482442488431074)
XLA Ops:
  8.5 1.7 fusion.66
  10.2 21.8 %while.24 = (s32[]{:T(128)}, f32[16,2048]{1,0:T(8,128)S(1)}, f32[16,8,2048]{2,1,0:T(8,128)S(1)}, f32[16,2048]{1,0:T(8,128)}, f32[16,8,2048]{2,1,0:T(8,128)S(1)},...) while((s32[]{:T(128)}, f32[16,2048]{1,0:T(8,128)S(1)}, ...), condition=%wide.region_2.3_spmd.clone, body=%wide.region_1.2_spmd.clone.sunk | while | flops 1114122 | bytes 789271 | solution.py:42
  34.0 28.0 %all-gather.6.cloned.1.call-done = f32[16,16,2048]{2,1,0:T(8,128)} async-done(((f32[2,16,2048]{2,1,0:T(8,128)}), f32[16,16,2048]{2,1,0:T(8,128)}) %all-gather.6.cloned.1.call-update) | async-done | bytes 2097168 | tf_op jit(solution)/shard_map/all_gather | solution.py:19
  61.9 1.6 fusion.69
  63.6 71.3 %while.23 = (s32[]{:T(128)}, f32[16,2048]{1,0:T(8,128)S(1)}, f32[16,8,2048]{2,1,0:T(8,128)}, f32[16,8,2048]{2,1,0:T(8,128)S(1)}, f32[16,2048]{1,0:T(8,128)}, /*i...) while((s32[]{:T(128)}, f32[16,2048]{1,0:T(8,128)S(1)}, ...), condition=%wide.region_12.13_spmd, body=%wide.region_3.12_spmd.sunk | while | flops 2408457 | bytes 2078409 | solution.py:57
  64.8 1.2 multiply_reduce_fusion.11
  69.3 1.2 multiply_reduce_fusion.11
  73.8 1.2 multiply_reduce_fusion.11
  78.2 1.2 multiply_reduce_fusion.11
  82.7 1.2 multiply_reduce_fusion.11
  87.1 1.2 multiply_reduce_fusion.11
  91.6 1.2 multiply_reduce_fusion.11
  96.0 1.2 multiply_reduce_fusion.11
  100.5 1.2 multiply_reduce_fusion.11
  104.9 1.2 multiply_reduce_fusion.11
  109.4 1.2 multiply_reduce_fusion.11
  113.8 1.2 multiply_reduce_fusion.11
  118.3 1.2 multiply_reduce_fusion.11
  122.7 1.2 multiply_reduce_fusion.11
  127.2 1.2 multiply_reduce_fusion.11
  134.9 1.5 fusion.64
  136.9 52.9 %all_to_all.10 = bf16[8,128,2048]{2,1,0:T(8,128)(2,1)S(1)} all-to-all(bf16[8,128,2048]{2,1,0:T(8,128)(2,1)S(1)} %stack.11), channel_id=1, replica_groups=mesh['dp'=4,'seq'=8,'expert'=4] {'seq'}, dimensions={0} | all-to-all | bytes 8388608 | tf_op jit(solution)/shard_map/all_to_all | solution.py:12
  190.4 1.6 copy-done.7
  192.0 6.0 %fusion.99 = f32[1024,1024]{1,0:T(8,128)} fusion(bf16[1024,2048]{1,0:T(8,128)(2,1)S(1)} %bitcast.416, bf16[2048,1024]{1,0:T(8,128)(2,1)S(1)} %copy-done.7), kind=kOutput, calls=%fused_computation.223 | convolution fusion | flops 4294967296 | bytes 12582912 | tf_op jit(solution)/shard_map/dot_general | solution.py:96
  198.0 46.3 %reduce-scatter.3.cloned.1.call-done = f32[256,1024]{1,0:T(8,128)} async-done(((f32[1024,1024]{1,0:T(8,128)}), f32[256,1024]{1,0:T(8,128)}) %reduce-scatter.3.cloned.1.call-update) | async-done | bytes 1048592 | tf_op jit(solution)/shard_map/reduce_scatter | solution.py:97
  244.3 4.4 all-to-all-start.1
  249.1 15.6 %all-to-all-done.1 = f32[8,32,1024]{2,1,0:T(8,128)S(1)} async-done(((f32[8,32,1024]{2,1,0:T(8,128)}), f32[8,32,1024]{2,1,0:T(8,128)S(1)}, u32[]{:S(2)}, u32[]{:S(2)}) %all-to-all-start.1) | async-done | bytes 1048608 | tf_op jit(solution)/shard_map/all_to_all | solution.py:99
  268.0 50.5 %all-gather.4.cloned.1.call-done = bf16[512,8192]{1,0:T(8,128)(2,1)} async-done(((bf16[16,8192]{1,0:T(8,128)(2,1)}), bf16[512,8192]{1,0:T(8,128)(2,1)}) %all-gather.4.cloned.1.call-update) | async-done | bytes 8388624 | tf_op jit(solution)/shard_map/all_gather | solution.py:132
  318.5 8.8 %fusion.100 = f32[512,384]{1,0:T(8,128)S(1)} fusion(bf16[512,8192]{1,0:T(8,128)(2,1)} %all-gather.4.cloned.1.call-done, bf16[8192,384]{1,0:T(8,128)(2,1)} %param.33), kind=kOutput, calls=%fused_computation.224 | convolution fusion | flops 3221225472 | bytes 15466496 | tf_op jit(solution)/shard_map/dot_general | solution.py:133
  327.3 17.1 %convolution_convert_fusion = bf16[512,8192]{1,0:T(8,128)(2,1)} fusion(bf16[384,8192]{1,0:T(8,128)(2,1)} %param.35, bf16[512,8192]{1,0:T(8,128)(2,1)} %all-gather.4.cloned.1.call-done, bf16[8192,384]{1,0:T(8,128)(2,1)} %param.34, f32[512,384]{1,0:T(8,128)S(1)} %fusion.100), kind=kOutput, calls=%fused_computation.132 | convolution fusion | flops 6447824896 | bytes 30146560 | tf_op jit(solution)/shard_map/dot_general | solution.py:137
  344.8 92.3 %reduce-scatter.5.cloned.1.call-done = bf16[16,8192]{1,0:T(8,128)(2,1)} async-done(((bf16[512,8192]{1,0:T(8,128)(2,1)}), bf16[16,8192]{1,0:T(8,128)(2,1)}) %reduce-scatter.5.cloned.1.call-update) | async-done | bytes 262160 | tf_op jit(solution)/shard_map/reduce_scatter | solution.py:136
  437.1 2.1 fusion.48
  (262 shorter events, 82.4 us)
Async XLA Ops:
  6.5 337.9 %copy-start = (bf16[8192,16]{0,1:T(8,128)(2,1)S(1)}, bf16[8192,16]{0,1:T(8,128)(2,1)}, u32[]{:S(2)}) copy-start(bf16[8192,16]{0,1:T(8,128)(2,1)} %param.31) | copy-start | bytes 786436
  6.5 27.3 %copy-start.5 = (bf16[16,128]{1,0:T(8,128)(2,1)S(1)}, bf16[16,128]{1,0:T(8,128)(2,1)}, u32[]{:S(2)}) copy-start(bf16[16,128]{1,0:T(8,128)(2,1)} %param.26) | copy-start | bytes 12292
  6.5 57.0 %copy-start.3 = (f32[2048]{0:T(1024)S(1)}, f32[2048]{0:T(1024)}, u32[]{:S(2)}) copy-start(f32[2048]{0:T(1024)} %param.27) | copy-start | bytes 24580
  6.5 55.4 %all-gather.6.cloned.1.call-start = ((), (), s32[]{:S(2)}) async-start(), calls=%async_computation.7 | async-start | bytes 2359296 | tf_op jit(solution)/shard_map/all_gather | solution.py:19
  33.7 210.6 %reduce-scatter.3.cloned.1.call-start = ((), (), s32[]{:S(2)}) async-start(), calls=%async_computation.4 | async-start | bytes 5242880 | tf_op jit(solution)/shard_map/reduce_scatter | solution.py:97
  63.5 71.3 %copy-start.2 = (bf16[128,2048]{1,0:T(8,128)(2,1)S(1)}, bf16[128,2048]{1,0:T(8,128)(2,1)}, u32[]{:S(2)}) copy-start(bf16[128,2048]{1,0:T(8,128)(2,1)} %param.21) | copy-start | bytes 1572868
  189.8 2.2 copy-start.7
  198.0 50.8 %copy-start.6 = (s32[32,2]{0,1:T(2,128)S(1)}, s32[32,2]{0,1:T(2,128)}, u32[]{:S(2)}) copy-start(s32[32,2]{0,1:T(2,128)} %param.32) | copy-start | bytes 772
  198.0 66.8 %copy-start.1 = (bf16[32,8192]{1,0:T(8,128)(2,1)S(1)}, bf16[32,8192]{1,0:T(8,128)(2,1)}, u32[]{:S(2)}) copy-start(bf16[32,8192]{1,0:T(8,128)(2,1)} %param.29) | copy-start | bytes 1572868
  198.0 67.1 %copy-start.4 = (f32[8192]{0:T(1024)S(1)}, f32[8192]{0:T(1024)}, u32[]{:S(2)}) copy-start(f32[8192]{0:T(1024)} %param.30) | copy-start | bytes 98308
  244.3 20.3 %all-to-all-start.1 = ((f32[8,32,1024]{2,1,0:T(8,128)}), f32[8,32,1024]{2,1,0:T(8,128)S(1)}, u32[]{:S(2)}, u32[]{:S(2)}) async-start(f32[8,32,1024]{2,1,0:T(8,128)} %bitcast.444), calls=%async_computation.2 | async-start | bytes 2097152 | tf_op jit(solution)/shard_map/all_to_all | solution.py:99
  248.7 69.8 %all-gather.4.cloned.1.call-start = ((), (), s32[]{:S(2)}) async-start(), calls=%async_computation.5 | async-start | bytes 8650752 | tf_op jit(solution)/shard_map/all_gather | solution.py:132
  267.8 169.3 %reduce-scatter.5.cloned.1.call-start = ((), (), s32[]{:S(2)}) async-start(), calls=%async_computation.6 | async-start | bytes 8650752 | tf_op jit(solution)/shard_map/reduce_scatter | solution.py:136
Sparse Core Ops, SparseCore 0:
  33.9 27.9 all-gather.5
  198.1 46.1 reduce-scatter.2
  267.9 50.6 all-gather.3
  344.6 92.4 reduce-scatter.4
